TPU v7x, 512 devices: a whole 4x8x8 slice. The times are simulated.
512 devices in a mesh: pp: 4 (over x_lo, core), cp: 16 (over z, x_hi), tp: 8 (over y).
Axes of the slice: x: 4 (x_hi: 2, x_lo: 2; x = x_hi * 2 + x_lo), y: 8, z: 8, core: 2. Of those that a mesh axis runs over, the one named last changes fastest.
Arguments:
- query: bfloat16 [4, 2048, 16384], P('pp', 'cp', 'tp'), may hold values from -200 to 200
- key: bfloat16 [4, 2048, 1024], P('pp', 'cp', 'tp'), may hold values from -6 to 6
- value: bfloat16 [4, 2048, 1024], P('pp', 'cp', 'tp'), may hold values from -6 to 6
- out_grad: bfloat16 [4, 2048, 16384], P('pp', 'cp', 'tp'), may hold values from -24 to 24
- lengths: int32 [6], replicated, may hold values from 1 to 1024, 2048 in all
- plan: int32 [16, 16], replicated, may hold values from 0 to 15, each once within a row
Outputs:
- handed_grad: bfloat16 [4, 2048, 16384], P('pp', 'cp', 'tp')
- key_grad: bfloat16 [4, 2048, 1024], P('pp', 'cp', 'tp')
- value_grad: bfloat16 [4, 2048, 1024], P('pp', 'cp', 'tp')
Inputs may be any that keep to these rules, and one draw needn't show every extreme that they name: Row s of plan is a permutation: for each of the blocks of 8 tokens of context shard s it names the shard that takes the block.
All inputs are finite; a program needn't handle non-finite values.
Results may differ from a plain program's by a relative error of at most 0.0085.
Values may be sent and summed in bfloat16 or wider, within the bound.
No kernel may reach another device: no remote copies, remote signals or barrier semaphores. Data moves between devices by JAX's collectives and lax.ppermute only.
A program may use at most 64 MiB of HBM per device.

v0:
```python
import jax
import jax.numpy as jnp
from jax import lax
from jax.sharding import PartitionSpec as P


def passed_along(array, axis, by):
    peers = lax.axis_size(axis)
    pairs = [(i, i + by) for i in range(peers) if 0 <= i + by < peers]
    return lax.ppermute(array, axis, pairs)


def attend(query_rows, grad_rows, query_pos, key_full, value_full, owner):
    tokens = query_rows.shape[0]
    head_width = key_full.shape[1]
    head_count = query_rows.shape[1] // head_width
    key_count = key_full.shape[0]
    total_rows = tokens * head_count
    score_scale = head_width ** (-0.5)
    flat_query = query_rows.reshape(total_rows, head_width)
    flat_grad = grad_rows.reshape(total_rows, head_width)
    row_pos = jnp.repeat(query_pos, head_count)
    row_doc = jnp.repeat(jnp.take(owner, query_pos), head_count)
    block_width = min(512, key_count)
    block_count = key_count // block_width
    key_pos = jnp.arange(key_count, dtype=jnp.int32)
    blocks = (
        key_full.reshape(block_count, block_width, head_width),
        value_full.reshape(block_count, block_width, head_width),
        key_pos.reshape(block_count, block_width),
        owner.reshape(block_count, block_width),
    )

    def masked_scores(key_block, pos_block, doc_block):
        scores = jnp.dot(flat_query, key_block.T, preferred_element_type=jnp.float32) * score_scale
        seen = (doc_block[None, :] == row_doc[:, None]) & (pos_block[None, :] <= row_pos[:, None])
        return jnp.where(seen, scores, -jnp.inf)

    def first_pass(state, block):
        top, total, weighted = state
        key_block, value_block, pos_block, doc_block = block
        scores = masked_scores(key_block, pos_block, doc_block)
        new_top = jnp.maximum(top, jnp.max(scores, axis=1))
        expo = jnp.exp(scores - new_top[:, None])
        shrink = jnp.exp(top - new_top)
        dprob = jnp.dot(flat_grad, value_block.T, preferred_element_type=jnp.float32)
        total = total * shrink + jnp.sum(expo, axis=1)
        weighted = weighted * shrink + jnp.sum(expo * dprob, axis=1)
        return ((new_top, total, weighted), None)

    start = (
        jnp.full((total_rows,), -1e30, jnp.float32),
        jnp.zeros((total_rows,), jnp.float32),
        jnp.zeros((total_rows,), jnp.float32),
    )
    (top, total, weighted), unused = lax.scan(first_pass, start, blocks)
    delta = weighted / total

    def second_pass(dquery, block):
        key_block, value_block, pos_block, doc_block = block
        scores = masked_scores(key_block, pos_block, doc_block)
        probs = jnp.exp(scores - top[:, None]) / total[:, None]
        dprob = jnp.dot(flat_grad, value_block.T, preferred_element_type=jnp.float32)
        probs_low = probs.astype(jnp.bfloat16)
        dscore = (probs * (dprob - delta[:, None]) * score_scale).astype(jnp.bfloat16)
        dvalue = jnp.dot(probs_low.T, flat_grad, preferred_element_type=jnp.float32)
        dkey = jnp.dot(dscore.T, flat_query, preferred_element_type=jnp.float32)
        dquery = dquery + jnp.dot(dscore, key_block, preferred_element_type=jnp.float32)
        return (dquery, jnp.concatenate([dkey, dvalue], axis=1))

    dquery, terms = lax.scan(second_pass, jnp.zeros((total_rows, head_width), jnp.float32), blocks)
    dquery = dquery.astype(jnp.bfloat16).reshape(tokens, head_count * head_width)
    return (dquery, terms.reshape(key_count, 2 * head_width))


def body(query, key, value, out_grad, lengths, plan):
    tokens = query.shape[1]
    width = query.shape[2]
    head_width = key.shape[2]
    shards = lax.axis_size("cp")
    own_index = lax.axis_index("cp")
    block_rows = tokens // shards
    key_full, value_full = (
        lax.all_gather(key[0], "cp", axis=0, tiled=True),
        lax.all_gather(value[0], "cp", axis=0, tiled=True),
    )
    key_count = key_full.shape[0]
    ends = jnp.cumsum(lengths)
    positions = jnp.arange(key_count, dtype=jnp.int32)
    owner = jnp.sum((positions[:, None] >= ends[None, :]).astype(jnp.int32), axis=1)
    iota = jnp.arange(shards, dtype=jnp.int32)
    inverse = jnp.sum(
        (plan[:, None, :] == iota[None, :, None]).astype(jnp.int32) * iota[None, None, :], axis=2
    )
    send_order = lax.dynamic_index_in_dim(inverse, own_index, 0, keepdims=False)

    def reorder(rows):
        grouped = rows.reshape(shards, block_rows, rows.shape[1])
        return jnp.take(grouped, send_order, axis=0)

    query_sent, grad_sent = (
        lax.all_to_all(reorder(query[0]), "cp", split_axis=0, concat_axis=0, tiled=True),
        lax.all_to_all(reorder(out_grad[0]), "cp", split_axis=0, concat_axis=0, tiled=True),
    )
    taken = lax.dynamic_index_in_dim(inverse, own_index, 1, keepdims=False)
    query_pos = (
        iota[:, None] * tokens
        + taken[:, None] * block_rows
        + jnp.arange(block_rows, dtype=jnp.int32)[None, :]
    ).reshape(tokens)
    dquery, terms = attend(
        query_sent.reshape(tokens, width),
        grad_sent.reshape(tokens, width),
        query_pos,
        key_full,
        value_full,
        owner,
    )
    handed = passed_along(dquery, "pp", -1)
    summed = lax.psum_scatter(terms, "cp", scatter_dimension=0, tiled=True)
    key_grad = summed[:, :head_width].astype(jnp.bfloat16)
    value_grad = summed[:, head_width:].astype(jnp.bfloat16)
    return (handed[None], key_grad[None], value_grad[None])


def solution(mesh):
    return jax.shard_map(
        body,
        mesh=mesh,
        in_specs=(
            P("pp", "cp", "tp"),
            P("pp", "cp", "tp"),
            P("pp", "cp", "tp"),
            P("pp", "cp", "tp"),
            P(),
            P(),
        ),
        out_specs=(P("pp", "cp", "tp"), P("pp", "cp", "tp"), P("pp", "cp", "tp")),
        check_vma=False,
    )
```

profile of v0, /device:TPU:8, one launch (start us, length us, event | category | flops | bytes accessed | tf_op | source)
XLA Modules:
  0.0 425.7 jit_solution(5239354460927206662)
XLA Ops:
  11.7 12.9 %all-to-all-start.1 = ((bf16[16,8,2048]{2,1,0:T(8,128)(2,1)}), bf16[16,8,2048]{2,1,0:T(8,128)(2,1)S(1)}, u32[]{:S(2)}, u32[]{:S(2)}) async-start(bf16[16,8,2048]{2,1,0:T(8,128)(2,1)} %get-tuple-element.306), calls=%async_computation.1 | async-start | bytes 1048576 | tf_op jit(solution)/shard_map/all_to_all | solution.py:103
  25.1 18.1 %all-to-all-done.1 = bf16[16,8,2048]{2,1,0:T(8,128)(2,1)S(1)} async-done(((bf16[16,8,2048]{2,1,0:T(8,128)(2,1)}), bf16[16,8,2048]{2,1,0:T(8,128)(2,1)S(1)}, u32[]{:S(2)}, u32[]{:S(2)}) %all-to-all-start.1) | async-done | bytes 524320 | tf_op jit(solution)/shard_map/all_to_all | solution.py:103
  43.2 3.6 all-to-all-start
  48.3 49.1 %all-gather = bf16[1,2048,128]{2,1,0:T(8,128)(2,1)} all-gather(bf16[1,128,128]{2,1,0:T(8,128)(2,1)S(1)} %copy-done.1), channel_id=2, replica_groups=mesh['pp'=4,'cp'=16,'tp'=8] {'cp'}, dimensions={1}, use_global_device_ids=true | all-gather | bytes 557056 | tf_op jit(solution)/shard_map/all_gather | solution.py:84
  97.4 43.7 %all-gather.1 = bf16[1,2048,128]{2,1,0:T(8,128)(2,1)} all-gather(bf16[1,128,128]{2,1,0:T(8,128)(2,1)S(1)} %copy-done.2), channel_id=3, replica_groups=mesh['pp'=4,'cp'=16,'tp'=8] {'cp'}, dimensions={1}, use_global_device_ids=true | all-gather | bytes 557056 | tf_op jit(solution)/shard_map/all_gather | solution.py:85
  142.4 20.0 %while.28 = (s32[]{:T(128)}, f32[2048]{0:T(1024)S(1)}, f32[2048]{0:T(1024)S(1)}, f32[2048]{0:T(1024)S(1)}, s32[4,512]{1,0:T(4,128)S(1)}, /*index=5*/s32[4,512]{1...) while((s32[]{:T(128)}, f32[2048]{0:T(1024)S(1)}, ...), condition=%wide.region_7.9_spmd.clone, body=%wide.region_3.0_spmd.clone.sunk | while | flops 548419584 | bytes 14120100 | solution.py:56
  142.8 2.2 fusion.69
  145.0 1.8 fusion.70
  147.8 2.2 fusion.69
  150.0 1.8 fusion.70
  152.8 2.2 fusion.69
  155.0 1.8 fusion.70
  157.8 2.2 fusion.69
  160.0 1.8 fusion.70
  162.5 41.5 %while.29 = (s32[]{:T(128)}, f32[2048,128]{1,0:T(8,128)S(1)}, f32[4,512,256]{2,1,0:T(8,128)}, s32[4,512]{1,0:T(4,128)S(1)}, s32[4,512]{1,0:T(4,128)S(1)}, /*inde...) while((s32[]{:T(128)}, f32[2048,128]{1,0:T(8,128)S(1)}, ...), condition=%wide.region_9.11_spmd.clone, body=%wide.region_8.10_spmd.clone.sunk | while | flops 1355415552 | bytes 27235516 | solution.py:71
  162.8 2.6 fusion.83
  166.3 1.6 fusion.84
  167.9 1.9 fusion.86
  169.8 2.0 convolution_add_fusion.2
  173.2 2.6 fusion.83
  176.6 1.6 fusion.84
  178.3 1.9 fusion.86
  180.2 2.0 convolution_add_fusion.2
  183.6 2.6 fusion.83
  188.7 1.9 fusion.86
  190.5 2.0 convolution_add_fusion.2
  194.0 2.6 fusion.83
  197.4 1.6 fusion.84
  199.1 1.9 fusion.86
  200.9 2.0 convolution_add_fusion.2
  205.6 2.5 collective-permute-done
  208.1 208.4 %reduce-scatter.2.cloned.1.call-done = f32[128,256]{1,0:T(8,128)} async-done(((f32[2048,256]{1,0:T(8,128)}), f32[128,256]{1,0:T(8,128)}) %reduce-scatter.2.cloned.1.call-update) | async-done | bytes 131088 | tf_op jit(solution)/shard_map/reduce_scatter | solution.py:120
  (116 shorter events, 26.3 us)
Async XLA Ops:
  7.2 1.2 copy-start
  7.2 17.4 %copy-start.3 = (s32[6]{0:T(128)S(1)}, s32[6]{0:T(128)}, u32[]{:S(2)}) copy-start(s32[6]{0:T(128)} %param.16) | copy-start | bytes 76
  7.2 41.1 %copy-start.1 = (bf16[1,128,128]{2,1,0:T(8,128)(2,1)S(1)}, bf16[1,128,128]{2,1,0:T(8,128)(2,1)}, u32[]{:S(2)}) copy-start(bf16[1,128,128]{2,1,0:T(8,128)(2,1)} %param.13) | copy-start | bytes 98308
  7.2 90.2 %copy-start.2 = (bf16[1,128,128]{2,1,0:T(8,128)(2,1)S(1)}, bf16[1,128,128]{2,1,0:T(8,128)(2,1)}, u32[]{:S(2)}) copy-start(bf16[1,128,128]{2,1,0:T(8,128)(2,1)} %param.14) | copy-start | bytes 98308
  11.7 31.5 %all-to-all-start.1 = ((bf16[16,8,2048]{2,1,0:T(8,128)(2,1)}), bf16[16,8,2048]{2,1,0:T(8,128)(2,1)S(1)}, u32[]{:S(2)}, u32[]{:S(2)}) async-start(bf16[16,8,2048]{2,1,0:T(8,128)(2,1)} %get-tuple-element.306), calls=%async_computation.1 | async-start | bytes 1048576 | tf_op jit(solution)/shard_map/all_to_all | solution.py:103
  43.2 98.1 %all-to-all-start = ((bf16[16,8,2048]{2,1,0:T(8,128)(2,1)}), bf16[16,8,2048]{2,1,0:T(8,128)(2,1)S(1)}, u32[]{:S(2)}, u32[]{:S(2)}) async-start(bf16[16,8,2048]{2,1,0:T(8,128)(2,1)} %get-tuple-element.307), calls=%async_computation | async-start | bytes 1048576 | tf_op jit(solution)/shard_map/all_to_all | solution.py:102
  46.8 369.7 %reduce-scatter.2.cloned.1.call-start = ((), (), s32[]{:S(2)}) async-start(), calls=%async_computation.3 | async-start | bytes 2228224 | tf_op jit(solution)/shard_map/reduce_scatter | solution.py:120
  204.3 3.8 collective-permute-start
Sparse Core Ops, SparseCore 0:
  204.1 212.3 reduce-scatter.1
where the time goes:
time: 427 us; the launch traced here: 426 us
  waiting for transfers between devices  229 us (54%)
  blocking collectives  92.8 us (22%)
  matrix products  51.4 us (12%)
  starting transfers between devices  17.8 us (4%)
  between operations  14.3 us (3%)
  local copies, waits for them, and re-layouts  13.4 us (3%)
  other arithmetic  6.55 us (2%)
    reduce_scatter x1, waiting for transfers between devices, body(): summed = lax.psum_scatter(terms, 'cp', scatter_dimension=0, tiled=True)  208 us
    all_gather x1, blocking collectives, body(): lax.all_gather(key[0], 'cp', axis=0, tiled=True)  49.1 us
    all_gather x1, blocking collectives, body(): lax.all_gather(value[0], 'cp', axis=0, tiled=True)  43.7 us
    dot_general x8, matrix products, masked_scores(): jnp.dot(flat_query, key_block.T, preferred_element_type=jnp.float32)  19 us
    all_to_all x1, waiting for transfers between devices, body(): lax.all_to_all(reorder(out_grad[0]), 'cp', split_axis=0, concat_axis=0, t...  18.1 us
    all_to_all x1, starting transfers between devices, body(): lax.all_to_all(reorder(out_grad[0]), 'cp', split_axis=0, concat_axis=0, t...  12.9 us
  transfers between devices with their start and end apart: 4, of which 3 were waited for; matrix products, arithmetic and copies ran while one was open for 1% of the time, Pallas kernels for 0%

commit v1 on v0

--- a/solution.py
+++ b/solution.py
@@ -81,7 +81,9 @@
     own_index = lax.axis_index("cp")
     block_rows = tokens // shards
     key_full, value_full = (
-        lax.all_gather(key[0], "cp", axis=0, tiled=True),
+        jnp.concatenate(
+            lax.all_to_all(jnp.stack([key[0]] * lax.axis_size("cp")), "cp", 0, 0), axis=0
+        ),
         lax.all_gather(value[0], "cp", axis=0, tiled=True),
     )
     key_count = key_full.shape[0]

time: 427 us -> 406 us (0.951)
  blocking collectives: 92.8 us -> 79.8 us
  starting transfers between devices: 17.8 us -> 9.14 us
    all_gather x1 -> x0, blocking collectives: 49.1 us -> none  [body(): lax.all_gather(key[0], 'cp', axis=0, tiled=True)]
    all_to_all x0 -> x1, blocking collectives: none -> 31.3 us  [body(): lax.all_to_all(reorder(out_grad[0]), 'cp', split_axis=0, concat_axis=0, t...]
    all_to_all x1, waiting for transfers between devices: 18.1 us -> 0.01 us  [body(): lax.all_to_all(jnp.stack([key[0]] * lax.axis_size('cp')), 'cp', 0, 0)]
    all_to_all x1, waiting for transfers between devices: 0.01 us -> 17.7 us  [body(): lax.all_to_all(reorder(query[0]), 'cp', split_axis=0, concat_axis=0, tile...]
    all_to_all x1, starting transfers between devices: 12.9 us -> 4.24 us  [body(): lax.all_to_all(jnp.stack([key[0]] * lax.axis_size('cp')), 'cp', 0, 0)]
    all_gather x1, blocking collectives: 43.7 us -> 48.4 us  [body(): lax.all_gather(value[0], 'cp', axis=0, tiled=True)]
where the time goes in v1:
time: 406 us; the launch traced here: 405 us
  waiting for transfers between devices  229 us (56%)
  blocking collectives  79.8 us (20%)
  matrix products  51.4 us (13%)
  local copies, waits for them, and re-layouts  14.3 us (4%)
  between operations  14.3 us (4%)
  starting transfers between devices  9.14 us (2%)
  other arithmetic  6.39 us (2%)
    reduce_scatter x1, waiting for transfers between devices, body(): summed = lax.psum_scatter(terms, 'cp', scatter_dimension=0, tiled=True)  209 us
    all_gather x1, blocking collectives, body(): lax.all_gather(value[0], 'cp', axis=0, tiled=True)  48.4 us
    all_to_all x1, blocking collectives, body(): lax.all_to_all(reorder(out_grad[0]), 'cp', split_axis=0, concat_axis=0, t...  31.3 us
    dot_general x8, matrix products, masked_scores(): jnp.dot(flat_query, key_block.T, preferred_element_type=jnp.float32)  19 us
    all_to_all x1, waiting for transfers between devices, body(): lax.all_to_all(reorder(query[0]), 'cp', split_axis=0, concat_axis=0, tile...  17.7 us
  transfers between devices with their start and end apart: 4, of which 3 were waited for; matrix products, arithmetic and copies ran while one was open for 1% of the time, Pallas kernels for 0%

profile of v1, /device:TPU:8, one launch (start us, length us, event | category | flops | bytes accessed | tf_op | source)
XLA Modules:
  0.0 404.7 jit_solution(10056897531075750914)
XLA Ops:
  11.5 31.3 %all_to_all.15 = bf16[16,8,2048]{2,1,0:T(8,128)(2,1)S(1)} all-to-all(bf16[16,8,2048]{2,1,0:T(8,128)(2,1)S(1)} %get-tuple-element.306), channel_id=1, replica_groups=mesh['pp'=4,'cp'=16,'tp'=8] {'cp'}, dimensions={0} | all-to-all | bytes 1048576 | tf_op jit(solution)/shard_map/all_to_all | solution.py:105
  42.9 3.6 all-to-all-start.1
  47.1 17.7 %all-to-all-done.1 = bf16[16,8,2048]{2,1,0:T(8,128)(2,1)S(1)} async-done(((bf16[16,8,2048]{2,1,0:T(8,128)(2,1)}), bf16[16,8,2048]{2,1,0:T(8,128)(2,1)S(1)}, u32[]{:S(2)}, u32[]{:S(2)}) %all-to-all-start.1) | async-done | bytes 524320 | tf_op jit(solution)/shard_map/all_to_all | solution.py:104
  65.7 4.2 %all-to-all-start = ((bf16[16,128,128]{2,1,0:T(8,128)(2,1)}), bf16[16,128,128]{2,1,0:T(8,128)(2,1)}, u32[]{:S(2)}, u32[]{:S(2)}) async-start(bf16[16,128,128]{2,1,0:T(8,128)(2,1)} %stack.3), calls=%async_computation | async-start | bytes 1048576 | tf_op jit(solution)/shard_map/all_to_all | solution.py:85
  71.3 48.4 %all-gather = bf16[1,2048,128]{2,1,0:T(8,128)(2,1)} all-gather(bf16[1,128,128]{2,1,0:T(8,128)(2,1)S(1)} %copy-done.2), channel_id=2, replica_groups=mesh['pp'=4,'cp'=16,'tp'=8] {'cp'}, dimensions={1}, use_global_device_ids=true | all-gather | bytes 557056 | tf_op jit(solution)/shard_map/all_gather | solution.py:87
  121.1 20.0 %while.28 = (s32[]{:T(128)}, f32[2048]{0:T(1024)S(1)}, f32[2048]{0:T(1024)S(1)}, f32[2048]{0:T(1024)S(1)}, s32[4,512]{1,0:T(4,128)S(1)}, /*index=5*/s32[4,512]{1...) while((s32[]{:T(128)}, f32[2048]{0:T(1024)S(1)}, ...), condition=%wide.region_7.9_spmd.clone, body=%wide.region_3.0_spmd.clone.sunk | while | flops 548419584 | bytes 14120100 | solution.py:56
  121.4 2.2 fusion.69
  123.6 1.8 fusion.70
  126.4 2.2 fusion.69
  128.6 1.8 fusion.70
  131.5 2.2 fusion.69
  133.7 1.8 fusion.70
  136.5 2.2 fusion.69
  138.7 1.8 fusion.70
  141.2 41.5 %while.29 = (s32[]{:T(128)}, f32[2048,128]{1,0:T(8,128)S(1)}, f32[4,512,256]{2,1,0:T(8,128)}, s32[4,512]{1,0:T(4,128)S(1)}, s32[4,512]{1,0:T(4,128)S(1)}, /*inde...) while((s32[]{:T(128)}, f32[2048,128]{1,0:T(8,128)S(1)}, ...), condition=%wide.region_9.11_spmd.clone, body=%wide.region_8.10_spmd.clone.sunk | while | flops 1355415552 | bytes 27235516 | solution.py:71
  141.5 2.6 fusion.83
  145.0 1.6 fusion.84
  146.6 1.9 fusion.86
  148.5 2.0 convolution_add_fusion.2
  151.9 2.6 fusion.83
  155.3 1.6 fusion.84
  156.9 1.9 fusion.86
  158.8 2.0 convolution_add_fusion.2
  162.2 2.6 fusion.83
  165.7 1.6 fusion.84
  167.3 1.9 fusion.86
  169.2 2.0 convolution_add_fusion.2
  172.6 2.6 fusion.83
  177.7 1.9 fusion.86
  179.6 2.0 convolution_add_fusion.2
  184.3 2.5 collective-permute-done
  186.8 208.8 %reduce-scatter.2.cloned.1.call-done = f32[128,256]{1,0:T(8,128)} async-done(((f32[2048,256]{1,0:T(8,128)}), f32[128,256]{1,0:T(8,128)}) %reduce-scatter.2.cloned.1.call-update) | async-done | bytes 131088 | tf_op jit(solution)/shard_map/reduce_scatter | solution.py:122
  (117 shorter events, 27.0 us)
Async XLA Ops:
  7.2 1.2 copy-start
  7.2 39.8 %copy-start.3 = (s32[6]{0:T(128)S(1)}, s32[6]{0:T(128)}, u32[]{:S(2)}) copy-start(s32[6]{0:T(128)} %param.16) | copy-start | bytes 76
  7.2 57.6 %copy-start.1 = (bf16[1,128,128]{2,1,0:T(8,128)(2,1)S(1)}, bf16[1,128,128]{2,1,0:T(8,128)(2,1)}, u32[]{:S(2)}) copy-start(bf16[1,128,128]{2,1,0:T(8,128)(2,1)} %param.13) | copy-start | bytes 98308
  8.3 63.0 %copy-start.2 = (bf16[1,128,128]{2,1,0:T(8,128)(2,1)S(1)}, bf16[1,128,128]{2,1,0:T(8,128)(2,1)}, u32[]{:S(2)}) copy-start(bf16[1,128,128]{2,1,0:T(8,128)(2,1)} %param.14) | copy-start | bytes 98308
  42.9 22.0 %all-to-all-start.1 = ((bf16[16,8,2048]{2,1,0:T(8,128)(2,1)}), bf16[16,8,2048]{2,1,0:T(8,128)(2,1)S(1)}, u32[]{:S(2)}, u32[]{:S(2)}) async-start(bf16[16,8,2048]{2,1,0:T(8,128)(2,1)} %get-tuple-element.307), calls=%async_computation.1 | async-start | bytes 1048576 | tf_op jit(solution)/shard_map/all_to_all | solution.py:104
  65.7 55.4 %all-to-all-start = ((bf16[16,128,128]{2,1,0:T(8,128)(2,1)}), bf16[16,128,128]{2,1,0:T(8,128)(2,1)}, u32[]{:S(2)}, u32[]{:S(2)}) async-start(bf16[16,128,128]{2,1,0:T(8,128)(2,1)} %stack.3), calls=%async_computation | async-start | bytes 1048576 | tf_op jit(solution)/shard_map/all_to_all | solution.py:85
  70.0 325.6 %reduce-scatter.2.cloned.1.call-start = ((), (), s32[]{:S(2)}) async-start(), calls=%async_computation.4 | async-start | bytes 2228224 | tf_op jit(solution)/shard_map/reduce_scatter | solution.py:122
  183.0 3.8 collective-permute-start
Sparse Core Ops, SparseCore 0:
  182.8 212.7 reduce-scatter.1
